TPU v7x, 32 devices: a whole 2x2x4 slice. The times are simulated.
32 devices in a mesh: seq: 4 (over y, x), tp: 8 (over z, core).
Axes of the slice: x: 2, y: 2, z: 4, core: 2. Of those that a mesh axis runs over, the one named last changes fastest.
Arguments:
- hidden: bfloat16 [512, 28672], P('seq', 'tp'), may hold values from -6 to 6
- down_weight: bfloat16 [28672, 8192], P('tp', 'seq'), may hold values from -0.03125 to 0.03125
- channel_scale: float32 [8192], P('seq'), may hold values from 0.25 to 1.75
Outputs:
- mixed: bfloat16 [512, 8192], P('tp', 'seq')
All inputs are finite; a program needn't handle non-finite values.
Results may differ from a plain program's by a relative error of at most 0.0049.
Values may be sent and summed in bfloat16 or wider, within the bound.
No kernel may reach another device: no remote copies, remote signals or barrier semaphores. Data moves between devices by JAX's collectives and lax.ppermute only.
A program may use at most 128 MiB of HBM per device.

v0:
```python
import math
import jax
import jax.numpy as jnp
import numpy as np
from jax import lax
from jax.sharding import PartitionSpec as P

PALEY = 28


def paley_table():
    residues = set((value * value % 13 for value in range(1, 13)))
    conference = np.zeros((14, 14))
    conference[0, 1:] = 1.0
    conference[1:, 0] = 1.0
    for first in range(13):
        for second in range(13):
            gap = (second - first) % 13
            if gap != 0:
                conference[1 + first, 1 + second] = 1.0 if gap in residues else -1.0
    upper = np.array([[1.0, 1.0], [1.0, -1.0]])
    lower = np.array([[1.0, -1.0], [-1.0, -1.0]])
    return np.kron(conference, upper) + np.kron(np.eye(14), lower)


def walsh_table(order):
    index_rows = np.arange(order)[:, None]
    index_cols = np.arange(order)[None, :]
    signs = np.ones((order, order))
    bit_value = 1
    while bit_value < order:
        both_set = index_rows // bit_value % 2 * (index_cols // bit_value % 2)
        signs = signs * (1 - 2 * both_set)
        bit_value = bit_value * 2
    return signs


def shards(hidden, down_weight, channel_scale):
    tp_count = lax.axis_size("tp")
    units = hidden.shape[1]
    total_units = units * tp_count
    local_table = jnp.asarray(np.kron(walsh_table(units // PALEY), paley_table()), jnp.bfloat16)
    factor = 1.0 / math.sqrt(total_units)
    spread = lax.all_to_all(hidden, "tp", split_axis=0, concat_axis=1, tiled=True)
    few_rows = spread.shape[0]
    blocks = spread.reshape(few_rows, tp_count, units)
    inner = jnp.einsum("rtl,lm->rtm", blocks, local_table, preferred_element_type=jnp.float32)
    cross_table = jnp.asarray(walsh_table(tp_count), jnp.float32)
    outer = jnp.einsum("rtm,tu->rum", inner, cross_table, precision=lax.Precision.HIGHEST)
    turned = (outer * factor).astype(jnp.bfloat16).reshape(few_rows, total_units)
    rotated = lax.all_to_all(turned, "tp", split_axis=1, concat_axis=0, tiled=True)
    partial_terms = jnp.dot(
        lax.all_gather(rotated, "seq", axis=0, tiled=True),
        down_weight,
        preferred_element_type=jnp.float32,
    )
    summed = lax.psum_scatter(partial_terms, "tp", scatter_dimension=0, tiled=True)
    return (summed * channel_scale[None, :]).astype(jnp.bfloat16)


def solution(mesh):
    placed = (P("seq", "tp"), P("tp", "seq"), P("seq"))
    return jax.shard_map(
        shards, mesh=mesh, in_specs=placed, out_specs=P("tp", "seq"), check_vma=False
    )
```

profile of v0, /device:TPU:0, one launch (start us, length us, event | category | flops | bytes accessed | tf_op | source)
XLA Modules:
  0.0 195.8 jit_solution(9701736656185318527)
XLA Ops:
  6.5 0.0 all-gather.2.cloned.1.call-start
  6.5 30.1 %all_to_all.32 = bf16[8,16,3584]{2,1,0:T(8,128)(2,1)S(1)} all-to-all(bf16[8,16,3584]{2,1,0:T(8,128)(2,1)} %bitcast.19), channel_id=1, replica_groups=mesh['seq'=4,'tp'=8] {'tp'}, dimensions={0} | all-to-all | bytes 1835008 | tf_op jit(solution)/shard_map/all_to_all | solution.py:44
  36.6 0.0 copy-start.1
  36.6 10.7 %convolution_bitcast_fusion = f32[16,8,3584]{2,1,0:T(8,128)S(1)} fusion(bf16[3584,3584,1]{1,0,2:T(8,128)(2,1)} %constant.8, bf16[8,16,3584]{2,1,0:T(8,128)(2,1)S(1)} %all_to_all.32), kind=kOutput, calls=%fused_computation.1 | convolution fusion | flops 3288334336 | bytes 28442624 | tf_op jit(solution)/shard_map/rtl,lm->rtm/dot_general | solution.py:47
  47.3 0.0 copy-done.1
  47.3 1.7 fusion.1
  49.0 0.3 copy.11
  49.3 26.9 %all_to_all.33 = bf16[16,8,3584]{2,0,1:T(8,128)(2,1)} all-to-all(bf16[16,8,3584]{2,0,1:T(8,128)(2,1)S(1)} %copy.11), channel_id=1, replica_groups=mesh['seq'=4,'tp'=8] {'tp'}, dimensions={1} | all-to-all | bytes 1835008 | tf_op jit(solution)/shard_map/all_to_all | solution.py:51
  76.2 0.0 all-gather.2.cloned.1.call-update
  76.2 0.0 reduce-scatter.2.cloned.1.call-start
  76.2 47.4 %all-gather.2.cloned.1.call-done = bf16[512,3584]{1,0:T(8,128)(2,1)} async-done(((bf16[128,3584]{1,0:T(8,128)(2,1)}), bf16[512,3584]{1,0:T(8,128)(2,1)}) %all-gather.2.cloned.1.call-update) | async-done | bytes 3670032 | tf_op jit(solution)/shard_map/all_gather | solution.py:53
  123.6 13.4 %fusion.2 = f32[512,2048]{1,0:T(8,128)} fusion(bf16[512,3584]{1,0:T(8,128)(2,1)} %all-gather.2.cloned.1.call-done, bf16[3584,2048]{1,0:T(8,128)(2,1)} %param.6), kind=kOutput, calls=%fused_computation.6 | convolution fusion | flops 7516192768 | bytes 22544384 | tf_op jit(solution)/shard_map/dot_general | solution.py:52
  137.0 0.0 copy-start
  137.0 0.0 reduce-scatter.2.cloned.1.call-update
  137.0 50.2 %reduce-scatter.2.cloned.1.call-done = f32[64,2048]{1,0:T(8,128)} async-done(((f32[512,2048]{1,0:T(8,128)}), f32[64,2048]{1,0:T(8,128)}) %reduce-scatter.2.cloned.1.call-update) | async-done | bytes 524304 | tf_op jit(solution)/shard_map/reduce_scatter | solution.py:57
  187.2 0.0 copy-done
  187.2 1.8 multiply_convert_fusion
Async XLA Ops:
  6.5 117.1 %all-gather.2.cloned.1.call-start = ((), (), s32[]{:S(2)}) async-start(), calls=%async_computation.3 | async-start | bytes 4587520 | tf_op jit(solution)/shard_map/all_gather | solution.py:53
  36.6 10.7 %copy-start.1 = (f32[8,8,1]{0,1,2:T(8,128)S(1)}, f32[8,8,1]{0,1,2:T(8,128)}, u32[]{:S(2)}) copy-start(f32[8,8,1]{0,1,2:T(8,128)} %constant.9) | copy-start | bytes 772
  76.2 111.0 %reduce-scatter.2.cloned.1.call-start = ((), (), s32[]{:S(2)}) async-start(), calls=%async_computation.4 | async-start | bytes 4718592 | tf_op jit(solution)/shard_map/reduce_scatter | solution.py:57
  137.0 50.2 %copy-start = (f32[2048]{0:T(1024)S(1)}, f32[2048]{0:T(1024)}, u32[]{:S(2)}) copy-start(f32[2048]{0:T(1024)} %param.7) | copy-start | bytes 24580
Sparse Core Ops, SparseCore 0:
  76.3 47.2 all-gather.1
  137.1 49.9 reduce-scatter.1
where the time goes:
time: 196 us
  waiting for transfers between devices  97.6 us (50%)
  blocking collectives  57 us (29%)
  matrix products  25.7 us (13%)
  between operations  13.4 us (7%)
    reduce_scatter x1, waiting for transfers between devices, shards(): lax.psum_scatter(partial_terms, 'tp', scatter_dimension=0, tiled=True)  50.2 us
    all_gather x1, waiting for transfers between devices, shards(): lax.all_gather(rotated, 'seq', axis=0, tiled=True)  47.4 us
    all_to_all x1, blocking collectives, shards(): lax.all_to_all(hidden, 'tp', split_axis=0, concat_axis=1, tiled=True)  30.1 us
    all_to_all x1, blocking collectives, shards(): lax.all_to_all(turned, 'tp', split_axis=1, concat_axis=0, tiled=True)  26.9 us
    dot_general x1, matrix products, shards(): jnp.dot(lax.all_gather(rotated, 'seq', axis=0, tiled=True), down_weight,...  13.4 us
    dot_general x1, matrix products, shards(): jnp.einsum('rtl,lm->rtm', blocks, local_table, preferred_element_type=jnp...  10.7 us
  transfers between devices with their start and end apart: 2, of which 2 were waited for; matrix products, arithmetic and copies ran while one was open for 0% of the time, Pallas kernels for 0%

commit v1 on v0

--- a/solution.py
+++ b/solution.py
@@ -6,6 +6,13 @@
 from jax.sharding import PartitionSpec as P
 
 PALEY = 28
+
+
+def stacked_exchange(array, axis, split, join):
+    peers = lax.axis_size(axis)
+    parts = jnp.stack(jnp.split(array, peers, axis=split), axis=0)
+    parts = lax.all_to_all(parts, axis, split_axis=0, concat_axis=0)
+    return jnp.concatenate(parts, axis=join)
 
 
 def paley_table():
@@ -41,7 +48,7 @@
     total_units = units * tp_count
     local_table = jnp.asarray(np.kron(walsh_table(units // PALEY), paley_table()), jnp.bfloat16)
     factor = 1.0 / math.sqrt(total_units)
-    spread = lax.all_to_all(hidden, "tp", split_axis=0, concat_axis=1, tiled=True)
+    spread = stacked_exchange(hidden, "tp", 0, 1)
     few_rows = spread.shape[0]
     blocks = spread.reshape(few_rows, tp_count, units)
     inner = jnp.einsum("rtl,lm->rtm", blocks, local_table, preferred_element_type=jnp.float32)

time: 196 us -> 203 us (1.036)
  local copies, waits for them, and re-layouts: 0.28 us -> 7.52 us
    unnamed x4 -> x11, local copies, waits for them, and re-layouts: 0.01 us -> 6.35 us
where the time goes in v1:
time: 203 us
  waiting for transfers between devices  97.5 us (48%)
  blocking collectives  56.8 us (28%)
  matrix products  25.6 us (13%)
  between operations  13.4 us (7%)
  local copies, waits for them, and re-layouts  7.52 us (4%)
    reduce_scatter x1, waiting for transfers between devices, shards(): lax.psum_scatter(partial_terms, 'tp', scatter_dimension=0, tiled=True)  50.2 us
    all_gather x1, waiting for transfers between devices, shards(): lax.all_gather(rotated, 'seq', axis=0, tiled=True)  47.3 us
    all_to_all x1, blocking collectives, stacked_exchange(): parts = lax.all_to_all(parts, axis, split_axis=0, concat_axis=0)  29.9 us
    all_to_all x1, blocking collectives, shards(): lax.all_to_all(turned, 'tp', split_axis=1, concat_axis=0, tiled=True)  26.9 us
    dot_general x1, matrix products, shards(): jnp.dot(lax.all_gather(rotated, 'seq', axis=0, tiled=True), down_weight,...  13.4 us
    dot_general x1, matrix products, shards(): jnp.einsum('rtl,lm->rtm', blocks, local_table, preferred_element_type=jnp...  10.6 us
    unnamed x11, local copies, waits for them, and re-layouts  6.35 us
  transfers between devices with their start and end apart: 2, of which 2 were waited for; matrix products, arithmetic and copies ran while one was open for 0% of the time, Pallas kernels for 0%

profile of v1, /device:TPU:0, one launch (start us, length us, event | category | flops | bytes accessed | tf_op | source)
XLA Modules:
  0.0 202.8 jit_solution(11129231996708976126)
XLA Ops:
  6.5 0.0 all-gather.2.cloned.1.call-start
  6.5 0.9 bitcast_dynamic-update-slice_fusion.7
  7.4 0.9 bitcast_dynamic-update-slice_fusion.6
  8.3 0.9 bitcast_dynamic-update-slice_fusion.5
  9.3 0.9 bitcast_dynamic-update-slice_fusion.4
  10.2 0.9 bitcast_dynamic-update-slice_fusion.3
  11.1 0.9 bitcast_dynamic-update-slice_fusion.2
  12.0 0.9 bitcast_dynamic-update-slice_fusion.1
  12.9 0.9 bitcast_dynamic-update-slice_fusion
  13.8 29.9 %all_to_all.21 = bf16[8,16,3584]{2,1,0:T(8,128)(2,1)S(1)} all-to-all(bf16[8,16,3584]{2,1,0:T(8,128)(2,1)S(1)} %bitcast_dynamic-update-slice_fusion), channel_id=1, replica_groups=mesh['seq'=4,'tp'=8] {'tp'}, dimensions={0} | all-to-all | bytes 1835008 | tf_op jit(solution)/shard_map/all_to_all | solution.py:14
  43.7 0.0 copy-start.1
  43.7 10.6 %fusion.2 = f32[16,8,3584]{2,1,0:T(8,128)S(1)} fusion(bf16[3584,3584,1]{1,0,2:T(8,128)(2,1)} %constant.8, bf16[8,16,3584]{2,1,0:T(8,128)(2,1)S(1)} %all_to_all.21), kind=kOutput, calls=%fused_computation.4 | convolution fusion | flops 3288334336 | bytes 28442624 | tf_op jit(solution)/shard_map/rtl,lm->rtm/dot_general | solution.py:54
  54.3 0.0 copy-done.1
  54.3 1.7 fusion.1
  56.0 0.3 copy.18
  56.2 26.9 %all_to_all.22 = bf16[16,8,3584]{2,0,1:T(8,128)(2,1)} all-to-all(bf16[16,8,3584]{2,0,1:T(8,128)(2,1)S(1)} %copy.18), channel_id=1, replica_groups=mesh['seq'=4,'tp'=8] {'tp'}, dimensions={1} | all-to-all | bytes 1835008 | tf_op jit(solution)/shard_map/all_to_all | solution.py:58
  83.1 0.0 all-gather.2.cloned.1.call-update
  83.2 0.0 reduce-scatter.2.cloned.1.call-start
  83.2 47.3 %all-gather.2.cloned.1.call-done = bf16[512,3584]{1,0:T(8,128)(2,1)} async-done(((bf16[128,3584]{1,0:T(8,128)(2,1)}), bf16[512,3584]{1,0:T(8,128)(2,1)}) %all-gather.2.cloned.1.call-update) | async-done | bytes 3670032 | tf_op jit(solution)/shard_map/all_gather | solution.py:60
  130.6 13.4 %fusion.3 = f32[512,2048]{1,0:T(8,128)} fusion(bf16[512,3584]{1,0:T(8,128)(2,1)} %all-gather.2.cloned.1.call-done, bf16[3584,2048]{1,0:T(8,128)(2,1)} %param.6), kind=kOutput, calls=%fused_computation.14 | convolution fusion | flops 7516192768 | bytes 22544384 | tf_op jit(solution)/shard_map/dot_general | solution.py:59
  143.9 0.0 copy-start
  143.9 0.0 reduce-scatter.2.cloned.1.call-update
  144.0 50.2 %reduce-scatter.2.cloned.1.call-done = f32[64,2048]{1,0:T(8,128)} async-done(((f32[512,2048]{1,0:T(8,128)}), f32[64,2048]{1,0:T(8,128)}) %reduce-scatter.2.cloned.1.call-update) | async-done | bytes 524304 | tf_op jit(solution)/shard_map/reduce_scatter | solution.py:64
  194.1 0.0 copy-done
  194.1 1.8 multiply_convert_fusion
Async XLA Ops:
  6.5 124.0 %all-gather.2.cloned.1.call-start = ((), (), s32[]{:S(2)}) async-start(), calls=%async_computation.3 | async-start | bytes 4587520 | tf_op jit(solution)/shard_map/all_gather | solution.py:60
  43.7 10.6 %copy-start.1 = (f32[8,8,1]{0,1,2:T(8,128)S(1)}, f32[8,8,1]{0,1,2:T(8,128)}, u32[]{:S(2)}) copy-start(f32[8,8,1]{0,1,2:T(8,128)} %constant.9) | copy-start | bytes 772
  83.2 111.0 %reduce-scatter.2.cloned.1.call-start = ((), (), s32[]{:S(2)}) async-start(), calls=%async_computation.4 | async-start | bytes 4718592 | tf_op jit(solution)/shard_map/reduce_scatter | solution.py:64
  143.9 50.2 %copy-start = (f32[2048]{0:T(1024)S(1)}, f32[2048]{0:T(1024)}, u32[]{:S(2)}) copy-start(f32[2048]{0:T(1024)} %param.7) | copy-start | bytes 24580
Sparse Core Ops, SparseCore 0:
  83.3 47.2 all-gather.1
  144.1 49.9 reduce-scatter.1
